TPU v7x, 32 devices: a whole 2x2x4 slice. The times are simulated.
32 devices in a mesh: row: 8 (over z, y), col: 4 (over x, core).
Axes of the slice: x: 2, y: 2, z: 4, core: 2. Of those that a mesh axis runs over, the one named last changes fastest.
Arguments:
- factor: float32 [4, 8, 256, 1024], P(None, 'row', None, 'col'), may hold values from -0.1875 to 0.1875
- rhs: float32 [4, 8, 256, 4096], P(None, 'row', None, 'col'), may hold values from -6 to 6
- diag_inv: float32 [4, 256, 256], replicated, may hold values from -0.5 to 1.3, as said below
Outputs:
- updated: float32 [4, 8, 256, 4096], P(None, 'row', None, 'col')
Inputs may be any that keep to these rules, and one draw needn't show every extreme that they name: Each diag_inv[k] is lower triangular with its diagonal between 0.7 and 1.3.
All inputs are finite; a program needn't handle non-finite values.
Results may differ from a plain program's by a relative error of at most 0.0001.
Values sent between devices are 32-bit elements; how exact they have to be, the bound alone decides.
No kernel may reach another device: no remote copies, remote signals or barrier semaphores. Data moves between devices by JAX's collectives and lax.ppermute only.
A program may use at most 64 MiB of HBM per device.

v0:
```python
import jax
import jax.numpy as jnp
from jax import lax
from jax.sharding import PartitionSpec as P

STEPS = 4


def broadcast(block, axis, holder):
    block = jnp.where(lax.axis_index(axis) == holder, block, jnp.zeros_like(block))
    return lax.psum(block, axis)


def matmul(left, right):
    return jnp.dot(left, right, precision=lax.Precision.HIGHEST, preferred_element_type=jnp.float32)


def per_device(factor, rhs, diag_inv):
    row_count = lax.axis_size("row")
    block_size = rhs.shape[2]
    local_blocks = rhs.shape[0]
    panel = lax.all_gather(factor, "col", axis=3, tiled=True)
    flat_panel = panel.reshape(local_blocks * block_size, STEPS * block_size)
    position = lax.axis_index("row")
    blocks = (jnp.arange(local_blocks, dtype=jnp.int32) * row_count + position)[:, None, None, None]
    work = rhs
    for step in range(STEPS):
        candidate = matmul(diag_inv[step], work[0, 0])
        solved = broadcast(candidate, "row", step)
        update = matmul(flat_panel[:, step * block_size : (step + 1) * block_size], solved).reshape(
            work.shape
        )
        work = jnp.where(
            blocks > step, work - update, jnp.where(blocks == step, solved[None, None], work)
        )
    return work


def solution(mesh):
    return jax.shard_map(
        per_device,
        mesh=mesh,
        in_specs=(P(None, "row", None, "col"), P(None, "row", None, "col"), P()),
        out_specs=P(None, "row", None, "col"),
        check_vma=False,
    )
```

profile of v0, /device:TPU:0, one launch (start us, length us, event | category | flops | bytes accessed | tf_op | source)
XLA Modules:
  0.0 394.6 jit_solution(5680344564141285933)
XLA Ops:
  7.4 0.0 all-reduce.5.cloned.1.call-start
  7.4 3.3 convolution_select_fusion.3
  10.7 0.0 all-reduce.5.cloned.1.call-update
  10.7 0.0 all-gather.2.cloned.1.call-start
  10.8 0.5 all-gather.2.cloned.1.call-update
  11.3 0.0 all-reduce.7.cloned.1.call-start
  11.4 81.4 %all-reduce.5.cloned.1.call-done = f32[256,1024]{1,0:T(8,128)} async-done(((f32[256,1024]{1,0:T(8,128)}), f32[256,1024]{1,0:T(8,128)}) %all-reduce.5.cloned.1.call-update) | async-done | bytes 1048592 | tf_op jit(solution)/shard_map/psum | solution.py:11
  92.7 0.0 copy-start.7
  92.7 0.0 all-gather.2.cloned.1.call-done
  92.7 0.0 copy-start.3
  92.7 5.4 %fusion.9 = f32[1024,1024]{0,1:T(8,128)S(1)} fusion(f32[256,1024]{1,0:T(8,128)} %all-reduce.5.cloned.1.call-done, f32[1024,1024]{1,0:T(8,128)} %bitcast.59), kind=kOutput, calls=%fused_computation.20 | convolution fusion | flops 3221225472 | bytes 6291456 | tf_op jit(solution)/shard_map/dot_general | solution.py:15
  98.1 0.0 copy-done.7
  98.1 0.0 copy-done.3
  98.2 0.0 copy-start.8
  98.2 1.6 select_select_fusion.3
  99.8 0.0 copy-start.1
  99.8 2.0 copy-done.1
  101.8 0.0 copy-done.8
  101.8 2.8 fusion.2
  104.7 0.0 all-reduce.7.cloned.1.call-update
  104.7 0.2 all-reduce.9.cloned.1.call-start
  104.9 77.8 %all-reduce.7.cloned.1.call-done = f32[256,1024]{0,1:T(8,128)} async-done(((f32[256,1024]{0,1:T(8,128)}), f32[256,1024]{0,1:T(8,128)}) %all-reduce.7.cloned.1.call-update) | async-done | bytes 1048592 | tf_op jit(solution)/shard_map/psum | solution.py:11
  182.7 0.0 copy-start.4
  182.7 7.1 %fusion.7 = f32[1024,1024]{0,1:T(8,128)} fusion(f32[256,1024]{0,1:T(8,128)} %all-reduce.7.cloned.1.call-done, f32[1024,1024]{1,0:T(8,128)} %bitcast.60), kind=kOutput, calls=%fused_computation.17 | convolution fusion | flops 3221225472 | bytes 6291456 | tf_op jit(solution)/shard_map/dot_general | solution.py:15
  189.8 0.0 copy-done.4
  189.8 0.3 copy.6
  190.2 4.7 %select_select_fusion.2 = f32[4,1,256,1024]{3,2,1,0:T(8,128)S(1)} fusion(f32[4,1,256,1024]{3,2,1,0:T(8,128)} %copy-done.1, f32[4,1,256,1024]{3,2,1,0:T(8,128)} %bitcast.56, f32[256,1024]{1,0:T(8,128)S(1)} %copy.6, pred[4]{0:T(512)(128)(4,1)S(1)} %get-tuple-element.7, pred[4]{0:T(512)(128)(4,1)S(1)} %get-tuple-element.8), kind=kLoop, calls=%fused_computation.2 | loop fusion | flops 3145728 | bytes 13631496 | tf_op jit(solution)/shard_map/jit(_where)/select_n | solution.py:33
  194.9 0.0 copy-start
  194.9 2.0 copy-done
  196.9 2.8 fusion.1
  199.8 0.0 all-reduce.9.cloned.1.call-update
  199.8 0.3 all-reduce.11.cloned.1.call-start
  200.1 77.8 %all-reduce.9.cloned.1.call-done = f32[256,1024]{0,1:T(8,128)} async-done(((f32[256,1024]{0,1:T(8,128)}), f32[256,1024]{0,1:T(8,128)}) %all-reduce.9.cloned.1.call-update) | async-done | bytes 1048592 | tf_op jit(solution)/shard_map/psum | solution.py:11
  277.9 0.0 copy-start.5
  277.9 7.1 %fusion.5 = f32[1024,1024]{0,1:T(8,128)} fusion(f32[256,1024]{0,1:T(8,128)} %all-reduce.9.cloned.1.call-done, f32[1024,1024]{1,0:T(8,128)} %bitcast.61), kind=kOutput, calls=%fused_computation.14 | convolution fusion | flops 3221225472 | bytes 6291456 | tf_op jit(solution)/shard_map/dot_general | solution.py:15
  285.0 0.0 copy-done.5
  285.0 0.3 copy.8
  285.4 4.7 %select_select_fusion.1 = f32[4,1,256,1024]{3,2,1,0:T(8,128)S(1)} fusion(f32[4,1,256,1024]{3,2,1,0:T(8,128)} %copy-done, f32[4,1,256,1024]{3,2,1,0:T(8,128)} %bitcast.57, f32[256,1024]{1,0:T(8,128)S(1)} %copy.8, pred[4]{0:T(512)(128)(4,1)S(1)} %get-tuple-element.9, pred[4]{0:T(512)(128)(4,1)S(1)} %get-tuple-element.10), kind=kLoop, calls=%fused_computation.1 | loop fusion | flops 3145728 | bytes 13631496 | tf_op jit(solution)/shard_map/jit(_where)/select_n | solution.py:33
  290.1 0.0 copy-start.2
  290.1 2.0 copy-done.2
  292.1 2.8 fusion
  295.0 0.0 all-reduce.11.cloned.1.call-update
  295.0 78.0 %all-reduce.11.cloned.1.call-done = f32[256,1024]{0,1:T(8,128)} async-done(((f32[256,1024]{0,1:T(8,128)}), f32[256,1024]{0,1:T(8,128)}) %all-reduce.11.cloned.1.call-update) | async-done | bytes 1048592 | tf_op jit(solution)/shard_map/psum | solution.py:11
  373.0 0.0 copy-start.6
  373.0 7.1 %fusion.3 = f32[1024,1024]{0,1:T(8,128)} fusion(f32[256,1024]{0,1:T(8,128)} %all-reduce.11.cloned.1.call-done, f32[1024,1024]{1,0:T(8,128)} %bitcast.62), kind=kOutput, calls=%fused_computation.11 | convolution fusion | flops 3221225472 | bytes 6291456 | tf_op jit(solution)/shard_map/dot_general | solution.py:15
  380.1 0.0 copy-done.6
  380.1 0.3 copy.10
  380.4 7.1 %select_select_fusion = f32[4,1,256,1024]{3,2,1,0:T(8,128)} fusion(f32[4,1,256,1024]{3,2,1,0:T(8,128)} %copy-done.2, f32[4,1,256,1024]{3,2,1,0:T(8,128)} %bitcast.55, f32[256,1024]{1,0:T(8,128)S(1)} %copy.10, pred[4]{0:T(512)(128)(4,1)S(1)} %get-tuple-element.11, pred[4]{0:T(512)(128)(4,1)S(1)} %get-tuple-element.12), kind=kLoop, calls=%fused_computation | loop fusion | flops 3145728 | bytes 13631496 | tf_op jit(solution)/shard_map/jit(_where)/select_n | solution.py:33
  (4 shorter events, 0.0 us)
Async XLA Ops:
  7.4 85.4 %all-reduce.5.cloned.1.call-start = ((), (), s32[]{:S(2)}) async-start(), calls=%async_computation | async-start | bytes 2097152 | tf_op jit(solution)/shard_map/psum | solution.py:11
  10.7 82.0 %all-gather.2.cloned.1.call-start = ((), (), s32[]{:S(2)}) async-start(), calls=%async_computation.1 | async-start | bytes 5242880 | tf_op jit(solution)/shard_map/all_gather | solution.py:22
  11.3 171.4 %all-reduce.7.cloned.1.call-start = ((), (), s32[]{:S(2)}) async-start(), calls=%async_computation.2 | async-start | bytes 2097152 | tf_op jit(solution)/shard_map/psum | solution.py:11
  92.7 5.4 %copy-start.7 = (f32[256,1024]{1,0:T(8,128)S(1)}, f32[256,1024]{1,0:T(8,128)}, u32[]{:S(2)}) copy-start(f32[256,1024]{1,0:T(8,128)} %all-reduce.5.cloned.1.call-done) | copy-start | bytes 3145732
  92.7 5.4 %copy-start.3 = (f32[4,1,256,1024]{3,2,1,0:T(8,128)S(1)}, f32[4,1,256,1024]{3,2,1,0:T(8,128)}, u32[]{:S(2)}) copy-start(f32[4,1,256,1024]{3,2,1,0:T(8,128)} %param.4) | copy-start | bytes 12582916
  98.2 3.7 copy-start.8
  99.8 2.0 copy-start.1
  104.7 173.2 %all-reduce.9.cloned.1.call-start = ((), (), s32[]{:S(2)}) async-start(), calls=%async_computation.3 | async-start | bytes 2097152 | tf_op jit(solution)/shard_map/psum | solution.py:11
  182.7 7.1 %copy-start.4 = (f32[256,1024]{0,1:T(8,128)S(1)}, f32[256,1024]{0,1:T(8,128)}, u32[]{:S(2)}) copy-start(f32[256,1024]{0,1:T(8,128)} %all-reduce.7.cloned.1.call-done) | copy-start | bytes 3145732
  194.9 2.0 copy-start
  199.8 173.2 %all-reduce.11.cloned.1.call-start = ((), (), s32[]{:S(2)}) async-start(), calls=%async_computation.4 | async-start | bytes 2097152 | tf_op jit(solution)/shard_map/psum | solution.py:11
  277.9 7.1 %copy-start.5 = (f32[256,1024]{0,1:T(8,128)S(1)}, f32[256,1024]{0,1:T(8,128)}, u32[]{:S(2)}) copy-start(f32[256,1024]{0,1:T(8,128)} %all-reduce.9.cloned.1.call-done) | copy-start | bytes 3145732
  290.1 2.0 copy-start.2
  373.0 7.1 %copy-start.6 = (f32[256,1024]{0,1:T(8,128)S(1)}, f32[256,1024]{0,1:T(8,128)}, u32[]{:S(2)}) copy-start(f32[256,1024]{0,1:T(8,128)} %all-reduce.11.cloned.1.call-done) | copy-start | bytes 3145732
Sparse Core Ops, SparseCore 0:
  11.7 81.0 all-reduce.4
  104.8 77.8 all-reduce.6
  199.9 77.9 all-reduce.8
  295.1 77.8 all-reduce.10
Sparse Core Ops, SparseCore 1:
  12.8 37.0 all-gather.1
where the time goes:
time: 395 us
  waiting for transfers between devices  316 us (80%)
  matrix products  38.6 us (10%)
  other arithmetic  18.2 us (5%)
  between operations  14.7 us (4%)
  local copies, waits for them, and re-layouts  7.04 us (2%)
    psum x4, waiting for transfers between devices, broadcast(): return lax.psum(block, axis)  315 us
    dot_general x8, matrix products, matmul(): jnp.dot(left, right, precision=lax.Precision.HIGHEST, preferred_element_t...  38.6 us
    select_n x4, other arithmetic, per_device(): jnp.where(blocks > step, work - update, jnp.where(blocks == step, solved[...  18.1 us
  transfers between devices with their start and end apart: 5, of which 4 were waited for; matrix products, arithmetic and copies ran while one was open for 0% of the time, Pallas kernels for 0%

commit v1 on v0

--- a/solution.py
+++ b/solution.py
@@ -8,7 +8,7 @@
 
 def broadcast(block, axis, holder):
     block = jnp.where(lax.axis_index(axis) == holder, block, jnp.zeros_like(block))
-    return lax.psum(block, axis)
+    return jnp.sum(lax.all_gather(block, axis), axis=0)
 
 
 def matmul(left, right):

time: 395 us -> 645 us (1.63)
  waiting for transfers between devices: 316 us -> 528 us
  local copies, waits for them, and re-layouts: 7.04 us -> 29.5 us
  other arithmetic: 18.2 us -> 30.3 us
    all_gather x0 -> x4, waiting for transfers between devices: none -> 498 us  [broadcast(): return jnp.sum(lax.all_gather(block, axis), axis=0)]
    psum x4 -> x0, waiting for transfers between devices: 315 us -> none  [broadcast(): return lax.psum(block, axis)]
    all_gather x1, waiting for transfers between devices: 0.01 us -> 29.8 us  [per_device(): panel = lax.all_gather(factor, 'col', axis=3, tiled=True)]
    unnamed x18 -> x13, local copies, waits for them, and re-layouts: 6.05 us -> 28.5 us
    reduce_sum x0 -> x4, other arithmetic: none -> 12.2 us  [broadcast(): return jnp.sum(lax.all_gather(block, axis), axis=0)]
  transfers between devices with their start and end apart: 5 -> 5, of which waited for: 4 -> 5; matrix products, arithmetic and copies ran while one was open for 0% -> 1% of each run, Pallas kernels for 0% -> 0%
where the time goes in v1:
time: 645 us; the launch traced here: 638 us
  waiting for transfers between devices  528 us (82%)
  matrix products  36.1 us (6%)
  other arithmetic  30.3 us (5%)
  local copies, waits for them, and re-layouts  29.5 us (5%)
  between operations  13.8 us (2%)
    all_gather x4, waiting for transfers between devices, broadcast(): return jnp.sum(lax.all_gather(block, axis), axis=0)  498 us
    dot_general x8, matrix products, matmul(): jnp.dot(left, right, precision=lax.Precision.HIGHEST, preferred_element_t...  36.1 us
    all_gather x1, waiting for transfers between devices, per_device(): panel = lax.all_gather(factor, 'col', axis=3, tiled=True)  29.8 us
    unnamed x13, local copies, waits for them, and re-layouts  28.5 us
    select_n x4, other arithmetic, per_device(): jnp.where(blocks > step, work - update, jnp.where(blocks == step, solved[...  18.1 us
  transfers between devices with their start and end apart: 5, of which 5 were waited for; matrix products, arithmetic and copies ran while one was open for 1% of the time, Pallas kernels for 0%

profile of v1, /device:TPU:0, one launch (start us, length us, event | category | flops | bytes accessed | tf_op | source)
XLA Modules:
  0.0 638.5 jit_solution(5260800671304562443)
XLA Ops:
  6.5 0.0 all-gather.12.cloned.1.call-start
  6.5 3.3 convolution_select_fusion.3
  9.9 0.0 all-gather.12.cloned.1.call-update
  9.9 0.0 all-gather.10.cloned.1.call-start
  9.9 0.7 all-gather.10.cloned.1.call-update
  10.6 0.0 all-gather.14.cloned.1.call-start
  10.7 126.5 %all-gather.12.cloned.1.call-done = f32[2048,1024]{1,0:T(8,128)} async-done(((f32[256,1024]{1,0:T(8,128)}), f32[2048,1024]{1,0:T(8,128)}) %all-gather.12.cloned.1.call-update) | async-done | bytes 8388624 | tf_op jit(solution)/shard_map/all_gather | solution.py:11
  137.2 4.4 reduce_sum.36
  141.6 29.8 %all-gather.10.cloned.1.call-done = f32[4,1,256,1024]{3,2,1,0:T(8,128)} async-done(((f32[4,1,256,256]{3,2,1,0:T(8,128)}), f32[4,1,256,1024]{3,2,1,0:T(8,128)}) %all-gather.10.cloned.1.call-update) | async-done | bytes 4194320 | tf_op jit(solution)/shard_map/all_gather | solution.py:22
  171.5 0.0 copy-start.3
  171.5 5.1 fusion.9
  176.5 0.0 copy-done.3
  176.5 0.0 copy-start.4
  176.6 1.6 select_select_fusion.3
  178.2 0.0 copy-start.1
  178.2 2.0 copy-done.1
  180.2 0.0 copy-done.4
  180.2 2.9 fusion.2
  183.1 0.0 all-gather.14.cloned.1.call-update
  183.2 0.2 all-gather.16.cloned.1.call-start
  183.4 124.9 %all-gather.14.cloned.1.call-done = f32[2048,1024]{0,1:T(8,128)} async-done(((f32[256,1024]{0,1:T(8,128)}), f32[2048,1024]{0,1:T(8,128)}) %all-gather.14.cloned.1.call-update) | async-done | bytes 8388624 | tf_op jit(solution)/shard_map/all_gather | solution.py:11
  308.2 7.5 %copy.15 = f32[128,8,8,256]{3,2,1,0:T(8,128)S(1)} copy(f32[128,8,8,256]{3,1,2,0:T(8,128)} %bitcast.76) | data formatting | bytes 16777216
  315.7 2.5 bitcast_reduce_fusion.2
  318.3 6.3 fusion.7
  324.6 0.3 copy.10
  324.9 4.7 select_select_fusion.2
  329.6 0.0 copy-start
  329.6 2.0 copy-done
  331.7 2.9 fusion.1
  334.6 0.0 all-gather.16.cloned.1.call-update
  334.6 0.3 all-gather.18.cloned.1.call-start
  334.9 123.0 %all-gather.16.cloned.1.call-done = f32[2048,1024]{0,1:T(8,128)} async-done(((f32[256,1024]{0,1:T(8,128)}), f32[2048,1024]{0,1:T(8,128)}) %all-gather.16.cloned.1.call-update) | async-done | bytes 8388624 | tf_op jit(solution)/shard_map/all_gather | solution.py:11
  457.9 7.5 %copy.16 = f32[128,8,8,256]{3,2,1,0:T(8,128)S(1)} copy(f32[128,8,8,256]{3,1,2,0:T(8,128)} %bitcast.77) | data formatting | bytes 16777216
  465.4 2.5 bitcast_reduce_fusion.1
  467.9 6.3 fusion.5
  474.2 0.3 copy.12
  474.5 4.7 select_select_fusion.1
  479.3 0.0 copy-start.2
  479.3 2.0 copy-done.2
  481.3 2.9 fusion
  484.2 0.0 all-gather.18.cloned.1.call-update
  484.2 123.3 %all-gather.18.cloned.1.call-done = f32[2048,1024]{0,1:T(8,128)} async-done(((f32[256,1024]{0,1:T(8,128)}), f32[2048,1024]{0,1:T(8,128)}) %all-gather.18.cloned.1.call-update) | async-done | bytes 8388624 | tf_op jit(solution)/shard_map/all_gather | solution.py:11
  607.5 7.5 %copy.17 = f32[128,8,8,256]{3,2,1,0:T(8,128)S(1)} copy(f32[128,8,8,256]{3,1,2,0:T(8,128)} %bitcast.78) | data formatting | bytes 16777216
  615.0 2.8 bitcast_reduce_fusion
  617.8 6.3 fusion.3
  624.1 0.3 copy.14
  624.4 7.1 %select_select_fusion = f32[4,1,256,1024]{3,2,1,0:T(8,128)} fusion(f32[4,1,256,1024]{3,2,1,0:T(8,128)} %copy-done.2, f32[4,1,256,1024]{3,2,1,0:T(8,128)} %bitcast.71, f32[256,1024]{1,0:T(8,128)S(1)} %copy.14, pred[4]{0:T(512)(128)(4,1)S(1)} %get-tuple-element.11, pred[4]{0:T(512)(128)(4,1)S(1)} %get-tuple-element.12), kind=kLoop, calls=%fused_computation.3 | loop fusion | flops 3145728 | bytes 13631496 | tf_op jit(solution)/shard_map/jit(_where)/select_n | solution.py:33
  (4 shorter events, 0.0 us)
Async XLA Ops:
  6.5 130.7 %all-gather.12.cloned.1.call-start = ((), (), s32[]{:S(2)}) async-start(), calls=%async_computation.1 | async-start | bytes 9437184 | tf_op jit(solution)/shard_map/all_gather | solution.py:11
  9.9 161.6 %all-gather.10.cloned.1.call-start = ((), (), s32[]{:S(2)}) async-start(), calls=%async_computation | async-start | bytes 5242880 | tf_op jit(solution)/shard_map/all_gather | solution.py:22
  10.6 297.6 %all-gather.14.cloned.1.call-start = ((), (), s32[]{:S(2)}) async-start(), calls=%async_computation.2 | async-start | bytes 9437184 | tf_op jit(solution)/shard_map/all_gather | solution.py:11
  171.5 5.1 copy-start.3
  176.5 3.7 copy-start.4
  178.2 2.0 copy-start.1
  183.2 274.7 %all-gather.16.cloned.1.call-start = ((), (), s32[]{:S(2)}) async-start(), calls=%async_computation.3 | async-start | bytes 9437184 | tf_op jit(solution)/shard_map/all_gather | solution.py:11
  329.6 2.0 copy-start
  334.6 272.9 %all-gather.18.cloned.1.call-start = ((), (), s32[]{:S(2)}) async-start(), calls=%async_computation.4 | async-start | bytes 9437184 | tf_op jit(solution)/shard_map/all_gather | solution.py:11
  479.3 2.0 copy-start.2
Sparse Core Ops, SparseCore 0:
  10.0 127.1 all-gather.11
  138.8 32.6 all-gather.9
  183.3 124.9 all-gather.13
  334.7 123.1 all-gather.15
  484.3 123.1 all-gather.17
